TPU v7x, 32 devices: a whole 2x2x4 slice. The times are simulated.
32 devices in a mesh: grad: 4 (over y, x), col: 8 (over z, core).
Axes of the slice: x: 2, y: 2, z: 4, core: 2. Of those that a mesh axis runs over, the one named last changes fastest.
Arguments:
- gradient: bfloat16 [16384, 53248], P(('grad', 'col'))
- test_matrix: bfloat16 [16384, 256], P(('grad', 'col')), may hold values from -6 to 6
Outputs:
- low_rank: float32 [16384, 256], P(('grad', 'col'))
- projector: float32 [53248, 256], P('col')
All inputs are finite; a program needn't handle non-finite values.
Results may differ from a plain program's by a relative error of at most 0.008.
Values may be sent and summed in bfloat16 or wider, within the bound.
No kernel may reach another device: no remote copies, remote signals or barrier semaphores. Data moves between devices by JAX's collectives and lax.ppermute only.
A program may use at most 256 MiB of HBM per device.

v0:
```python
import math
import jax
import jax.numpy as jnp
from jax import lax
from jax.sharding import PartitionSpec as P

FF = 53248
POWER = 2


def orthonormal(matrix, reduce_gram):
    partial_gram = lax.dot_general(
        matrix,
        matrix,
        (((0,), (0,)), ((), ())),
        precision=lax.Precision.HIGHEST,
        preferred_element_type=jnp.float32,
    )
    gram = reduce_gram(partial_gram)
    lower_factor = jnp.linalg.cholesky(gram)
    return lax.linalg.triangular_solve(
        lower_factor, matrix, left_side=False, lower=True, transpose_a=True
    )


def gram_over_columns(partial_gram):
    return lax.psum(partial_gram, "col")


def shards(gradient, test_matrix):
    blocks = lax.all_to_all(gradient, "col", split_axis=1, concat_axis=0, tiled=True)

    def add_sketch(row_piece):
        return lax.dot_general(
            blocks, row_piece, (((0,), (0,)), ((), ())), preferred_element_type=jnp.float32
        )

    sketch = add_sketch(lax.all_gather(test_matrix, "col", axis=0, tiled=True))
    for iteration in range(POWER + 1):
        summed = lax.psum(sketch, "grad")
        basis_block = orthonormal(summed, gram_over_columns)
        basis_bf = basis_block.astype(jnp.bfloat16)
        reduced = lax.psum_scatter(
            jnp.dot(blocks, basis_bf, preferred_element_type=jnp.float32),
            "col",
            scatter_dimension=0,
            tiled=True,
        )
        if iteration < POWER:
            reduced_bf = reduced.astype(jnp.bfloat16)
            sketch = add_sketch(lax.all_gather(reduced_bf, "col", axis=0, tiled=True))
    return (reduced, basis_block * math.sqrt(FF))


def solution(mesh):
    return jax.shard_map(
        shards,
        mesh=mesh,
        in_specs=(P(("grad", "col"), None), P(("grad", "col"), None)),
        out_specs=(P(("grad", "col"), None), P("col", None)),
        check_vma=False,
    )
```

profile of v0, /device:TPU:0, one launch (start us, length us, event | category | flops | bytes accessed | tf_op | source)
XLA Modules:
  0.0 2602.8 jit_solution(11232503956803364355)
XLA Ops:
  7.2 70.6 %copy.20 = bf16[512,53248]{0,1:T(8,128)(2,1)} copy(bf16[512,53248]{1,0:T(8,128)(2,1)} %param.5) | data formatting | bytes 109051904 | tf_op args[0]
  87.4 1189.5 %all-to-all-done = bf16[512,8,6656]{0,2,1:T(8,128)(2,1)} async-done(((bf16[512,8,6656]{0,2,1:T(8,128)(2,1)}), bf16[512,8,6656]{0,2,1:T(8,128)(2,1)}, u32[]{:S(2)}, u32[]{:S(2)}) %all-to-all-start) | async-done | bytes 54525984 | tf_op jit(solution)/shard_map/all_to_all | solution.py:31
  1276.9 64.6 %copy.21 = bf16[8,512,6656]{2,1,0:T(8,128)(2,1)} copy(bf16[8,512,6656]{1,2,0:T(8,128)(2,1)} %bitcast.1) | data formatting | bytes 109051904 | tf_op jit(solution)/shard_map/all_to_all | solution.py:31
  1341.5 25.8 fusion.41
  1367.7 146.1 %all-reduce.8.cloned.1.call-done = f32[6656,256]{1,0:T(8,128)} async-done(((f32[6656,256]{1,0:T(8,128)}), f32[6656,256]{1,0:T(8,128)}) %all-reduce.8.cloned.1.call-update) | async-done | bytes 6815760 | tf_op jit(solution)/shard_map/psum | solution.py:40
  1513.8 16.6 fusion.42
  1531.0 55.0 %all-reduce.10.cloned.1.call-done = f32[256,256]{0,1:T(8,128)} async-done(((f32[256,256]{0,1:T(8,128)}), f32[256,256]{0,1:T(8,128)}) %all-reduce.10.cloned.1.call-update) | async-done | bytes 262160 | tf_op jit(solution)/shard_map/psum | solution.py:27
  1588.1 11.7 cholesky.172
  1610.2 11.7 cholesky.189
  1628.9 19.7 custom-call.16
  1664.7 24.3 convolution_bitcast_fusion.4
  1689.1 49.1 %reduce-scatter.4.cloned.1.call-done = f32[512,256]{0,1:T(8,128)} async-done(((f32[4096,256]{0,1:T(8,128)}), f32[512,256]{0,1:T(8,128)}) %reduce-scatter.4.cloned.1.call-update) | async-done | bytes 524304 | tf_op jit(solution)/shard_map/reduce_scatter | solution.py:43
  1740.1 27.8 %all-gather.6.cloned.1.call-done = bf16[4096,256]{0,1:T(8,128)(2,1)} async-done(((bf16[512,256]{0,1:T(8,128)(2,1)}), bf16[4096,256]{0,1:T(8,128)(2,1)}) %all-gather.6.cloned.1.call-update) | async-done | bytes 2097168 | tf_op jit(solution)/shard_map/all_gather | solution.py:51
  1767.9 25.5 convolution_bitcast_fusion.1
  1793.5 146.3 %all-reduce.12.cloned.1.call-done = f32[6656,256]{0,1:T(8,128)} async-done(((f32[6656,256]{0,1:T(8,128)}), f32[6656,256]{0,1:T(8,128)}) %all-reduce.12.cloned.1.call-update) | async-done | bytes 6815760 | tf_op jit(solution)/shard_map/psum | solution.py:40
  1939.8 19.3 fusion.43
  1959.6 55.1 %all-reduce.14.cloned.1.call-done = f32[256,256]{0,1:T(8,128)} async-done(((f32[256,256]{0,1:T(8,128)}), f32[256,256]{0,1:T(8,128)}) %all-reduce.14.cloned.1.call-update) | async-done | bytes 262160 | tf_op jit(solution)/shard_map/psum | solution.py:27
  2016.8 11.7 cholesky.206
  2038.9 11.7 cholesky.223
  2058.1 19.7 custom-call.18
  2091.4 24.5 convolution_bitcast_fusion.3
  2116.0 49.1 %reduce-scatter.6.cloned.1.call-done = f32[512,256]{0,1:T(8,128)} async-done(((f32[4096,256]{0,1:T(8,128)}), f32[512,256]{0,1:T(8,128)}) %reduce-scatter.6.cloned.1.call-update) | async-done | bytes 524304 | tf_op jit(solution)/shard_map/reduce_scatter | solution.py:43
  2167.0 28.0 %all-gather.8.cloned.1.call-done = bf16[4096,256]{0,1:T(8,128)(2,1)} async-done(((bf16[512,256]{0,1:T(8,128)(2,1)}), bf16[4096,256]{0,1:T(8,128)(2,1)}) %all-gather.8.cloned.1.call-update) | async-done | bytes 2097168 | tf_op jit(solution)/shard_map/all_gather | solution.py:51
  2194.9 25.5 convolution_bitcast_fusion
  2220.5 146.3 %all-reduce.16.cloned.1.call-done = f32[6656,256]{0,1:T(8,128)} async-done(((f32[6656,256]{0,1:T(8,128)}), f32[6656,256]{0,1:T(8,128)}) %all-reduce.16.cloned.1.call-update) | async-done | bytes 6815760 | tf_op jit(solution)/shard_map/psum | solution.py:40
  2366.8 19.3 fusion.44
  2386.6 55.1 %all-reduce.18.cloned.1.call-done = f32[256,256]{0,1:T(8,128)} async-done(((f32[256,256]{0,1:T(8,128)}), f32[256,256]{0,1:T(8,128)}) %all-reduce.18.cloned.1.call-update) | async-done | bytes 262160 | tf_op jit(solution)/shard_map/psum | solution.py:27
  2443.9 11.7 cholesky.240
  2465.9 11.7 cholesky.257
  2485.2 19.7 custom-call.20
  2519.2 25.4 convolution_bitcast_fusion.2
  2558.0 35.7 %reduce-scatter.8.cloned.1.call-done = f32[512,256]{0,1:T(8,128)} async-done(((f32[4096,256]{0,1:T(8,128)}), f32[512,256]{0,1:T(8,128)}) %reduce-scatter.8.cloned.1.call-update) | async-done | bytes 524304 | tf_op jit(solution)/shard_map/reduce_scatter | solution.py:43
  (113 shorter events, 142.1 us)
Async XLA Ops:
  77.8 1199.1 %all-to-all-start = ((bf16[512,8,6656]{0,2,1:T(8,128)(2,1)}), bf16[512,8,6656]{0,2,1:T(8,128)(2,1)}, u32[]{:S(2)}, u32[]{:S(2)}) async-start(bf16[512,8,6656]{0,2,1:T(8,128)(2,1)} %bitcast.124), calls=%async_computation | async-start | bytes 109051904 | tf_op jit(solution)/shard_map/all_to_all | solution.py:31
  86.6 1254.9 %all-gather.4.cloned.1.call-start = ((), (), s32[]{:S(2)}) async-start(), calls=%async_computation.4 | async-start | bytes 2359296 | tf_op jit(solution)/shard_map/all_gather | solution.py:38
  87.3 1426.5 %all-reduce.8.cloned.1.call-start = ((), (), s32[]{:S(2)}) async-start(), calls=%async_computation.5 | async-start | bytes 13631488 | tf_op jit(solution)/shard_map/psum | solution.py:40
  1367.4 218.6 %all-reduce.10.cloned.1.call-start = ((), (), s32[]{:S(2)}) async-start(), calls=%async_computation.6 | async-start | bytes 524288 | tf_op jit(solution)/shard_map/psum | solution.py:27
  1530.4 207.8 %reduce-scatter.4.cloned.1.call-start = ((), (), s32[]{:S(2)}) async-start(), calls=%async_computation.7 | async-start | bytes 4718592 | tf_op jit(solution)/shard_map/reduce_scatter | solution.py:43
  1628.2 0.7 copy-start.4
  1648.5 5.2 copy-start
  1689.1 78.8 %all-gather.6.cloned.1.call-start = ((), (), s32[]{:S(2)}) async-start(), calls=%async_computation.8 | async-start | bytes 2359296 | tf_op jit(solution)/shard_map/all_gather | solution.py:51
  1740.0 199.8 %all-reduce.12.cloned.1.call-start = ((), (), s32[]{:S(2)}) async-start(), calls=%async_computation.9 | async-start | bytes 13631488 | tf_op jit(solution)/shard_map/psum | solution.py:40
  1793.4 221.3 %all-reduce.14.cloned.1.call-start = ((), (), s32[]{:S(2)}) async-start(), calls=%async_computation.10 | async-start | bytes 524288 | tf_op jit(solution)/shard_map/psum | solution.py:27
  1959.1 206.0 %reduce-scatter.6.cloned.1.call-start = ((), (), s32[]{:S(2)}) async-start(), calls=%async_computation.11 | async-start | bytes 4718592 | tf_op jit(solution)/shard_map/reduce_scatter | solution.py:43
  2057.4 0.7 copy-start.5
  2077.8 5.2 copy-start.2
  2116.0 79.0 %all-gather.8.cloned.1.call-start = ((), (), s32[]{:S(2)}) async-start(), calls=%async_computation.12 | async-start | bytes 2359296 | tf_op jit(solution)/shard_map/all_gather | solution.py:51
  2166.9 199.9 %all-reduce.16.cloned.1.call-start = ((), (), s32[]{:S(2)}) async-start(), calls=%async_computation.13 | async-start | bytes 13631488 | tf_op jit(solution)/shard_map/psum | solution.py:40
  2220.5 221.3 %all-reduce.18.cloned.1.call-start = ((), (), s32[]{:S(2)}) async-start(), calls=%async_computation.14 | async-start | bytes 524288 | tf_op jit(solution)/shard_map/psum | solution.py:27
  2386.2 207.5 %reduce-scatter.8.cloned.1.call-start = ((), (), s32[]{:S(2)}) async-start(), calls=%async_computation.15 | async-start | bytes 4718592 | tf_op jit(solution)/shard_map/reduce_scatter | solution.py:43
  2484.5 0.7 copy-start.3
  2504.9 5.2 copy-start.1
Sparse Core Ops, SparseCore 0:
  89.0 49.5 all-gather.3
  1367.5 146.2 all-reduce.7
  1530.6 55.4 all-reduce.9
  1689.2 48.9 reduce-scatter.3
  1740.2 27.5 all-gather.5
  1793.5 146.1 all-reduce.11
  1959.2 55.4 all-reduce.13
  2116.1 48.9 reduce-scatter.5
  2167.3 27.6 all-gather.7
  2220.6 146.1 all-reduce.15
  2386.3 55.4 all-reduce.17
  2544.7 48.9 reduce-scatter.7
where the time goes:
time: 2610 us; the launch traced here: 2600 us
  waiting for transfers between devices  1980 us (76%)
  matrix products  252 us (10%)
  other arithmetic  174 us (7%)
  local copies, waits for them, and re-layouts  163 us (6%)
    all_to_all x1, waiting for transfers between devices, shards(): lax.all_to_all(gradient, 'col', split_axis=1, concat_axis=0, tiled=True)  1190 us
    psum x3, waiting for transfers between devices, shards(): summed = lax.psum(sketch, 'grad')  439 us
    psum x3, waiting for transfers between devices, gram_over_columns(): return lax.psum(partial_gram, 'col')  165 us
    reduce_scatter x3, waiting for transfers between devices, shards(): lax.psum_scatter(jnp.dot(blocks, basis_bf, preferred_element_type=jnp.flo...  134 us
    another operation x20, other arithmetic, orthonormal(): lower_factor = jnp.linalg.cholesky(gram)  103 us
    unnamed x15, local copies, waits for them, and re-layouts  82.9 us
    dot_general x3, matrix products, add_sketch(): lax.dot_general(blocks, row_piece, (((0,), (0,)), ((), ())), preferred_el...  76.9 us
    dot_general x3, matrix products, shards(): jnp.dot(blocks, basis_bf, preferred_element_type=jnp.float32)  74.2 us
  transfers between devices with their start and end apart: 13, of which 12 were waited for; matrix products, arithmetic and copies ran while one was open for 3% of the time, Pallas kernels for 0%

commit v1 on v0

--- a/solution.py
+++ b/solution.py
@@ -28,7 +28,16 @@
 
 
 def shards(gradient, test_matrix):
-    blocks = lax.all_to_all(gradient, "col", split_axis=1, concat_axis=0, tiled=True)
+    _expand_positions = lambda frame: jnp.concatenate(
+        lax.all_to_all(
+            jnp.stack(jnp.split(frame, lax.axis_size("col"), axis=1), 0),
+            axis_name="col",
+            split_axis=0,
+            concat_axis=0,
+        ),
+        0,
+    )
+    blocks = _expand_positions(gradient)
 
     def add_sketch(row_piece):
         return lax.dot_general(

time: 2610 us -> 2520 us (0.966)
  local copies, waits for them, and re-layouts: 163 us -> 74.9 us
    all_to_all x1 -> x0, local copies, waits for them, and re-layouts: 64.6 us -> none  [shards(): lax.all_to_all(gradient, 'col', split_axis=1, concat_axis=0, tiled=True)]
    all_to_all x1, waiting for transfers between devices: 1190 us -> 1140 us  [shards(): lax.all_to_all(jnp.stack(jnp.split(frame, lax.axis_size('col'), axis=1),...]
    all_gather x1, waiting for transfers between devices: 0.01 us -> 51.2 us  [shards(): sketch = add_sketch(lax.all_gather(test_matrix, 'col', axis=0, tiled=True))]
    unnamed x15 -> x20, local copies, waits for them, and re-layouts: 82.9 us -> 53.5 us
  transfers between devices with their start and end apart: 13 -> 13, of which waited for: 12 -> 13; matrix products, arithmetic and copies ran while one was open for 3% -> 1% of each run, Pallas kernels for 0% -> 0%
where the time goes in v1:
time: 2520 us; the launch traced here: 2510 us
  waiting for transfers between devices  1980 us (79%)
  matrix products  250 us (10%)
  other arithmetic  174 us (7%)
  local copies, waits for them, and re-layouts  74.9 us (3%)
    all_to_all x1, waiting for transfers between devices, shards(): lax.all_to_all(jnp.stack(jnp.split(frame, lax.axis_size('col'), axis=1),...  1140 us
    psum x3, waiting for transfers between devices, shards(): summed = lax.psum(sketch, 'grad')  439 us
    psum x3, waiting for transfers between devices, gram_over_columns(): return lax.psum(partial_gram, 'col')  166 us
    reduce_scatter x3, waiting for transfers between devices, shards(): lax.psum_scatter(jnp.dot(blocks, basis_bf, preferred_element_type=jnp.flo...  134 us
    another operation x20, other arithmetic, orthonormal(): lower_factor = jnp.linalg.cholesky(gram)  103 us
    dot_general x3, matrix products, add_sketch(): lax.dot_general(blocks, row_piece, (((0,), (0,)), ((), ())), preferred_el...  77.5 us
    dot_general x3, matrix products, shards(): jnp.dot(blocks, basis_bf, preferred_element_type=jnp.float32)  71.9 us
    another operation x7, other arithmetic, orthonormal(): lax.linalg.triangular_solve(lower_factor, matrix, left_side=False, lower=...  59.3 us
  transfers between devices with their start and end apart: 13, of which 13 were waited for; matrix products, arithmetic and copies ran while one was open for 1% of the time, Pallas kernels for 0%

profile of v1, /device:TPU:0, one launch (start us, length us, event | category | flops | bytes accessed | tf_op | source)
XLA Modules:
  0.0 2513.4 jit_solution(13879430882355785849)
XLA Ops:
  66.3 51.2 %all-gather.4.cloned.1.call-done = bf16[4096,256]{1,0:T(8,128)(2,1)} async-done(((bf16[512,256]{1,0:T(8,128)(2,1)}), bf16[4096,256]{1,0:T(8,128)(2,1)}) %all-gather.4.cloned.1.call-update) | async-done | bytes 2097168 | tf_op jit(solution)/shard_map/all_gather | solution.py:47
  117.5 1138.3 %all-to-all-done = bf16[8,512,6656]{2,1,0:T(8,128)(2,1)} async-done(((bf16[8,512,6656]{2,1,0:T(8,128)(2,1)}), bf16[8,512,6656]{2,1,0:T(8,128)(2,1)}, u32[]{:S(2)}, u32[]{:S(2)}) %all-to-all-start) | async-done | bytes 54525984 | tf_op jit(solution)/shard_map/all_to_all | solution.py:32
  1255.8 25.8 %fusion.44 = f32[6656,256]{1,0:T(8,128)} fusion(bf16[4096,6656]{1,0:T(8,128)(2,1)} %bitcast.8, bf16[4096,256]{1,0:T(8,128)(2,1)} %all-gather.4.cloned.1.call-done), kind=kOutput, calls=%fused_computation.99 | convolution fusion | flops 13958643712 | bytes 63438848 | tf_op jit(solution)/shard_map/dot_general | solution.py:43
  1282.2 145.9 %all-reduce.8.cloned.1.call-done = f32[6656,256]{1,0:T(8,128)} async-done(((f32[6656,256]{1,0:T(8,128)}), f32[6656,256]{1,0:T(8,128)}) %all-reduce.8.cloned.1.call-update) | async-done | bytes 6815760 | tf_op jit(solution)/shard_map/psum | solution.py:49
  1428.1 16.6 fusion.45
  1444.9 55.3 %all-reduce.10.cloned.1.call-done = f32[256,256]{0,1:T(8,128)} async-done(((f32[256,256]{0,1:T(8,128)}), f32[256,256]{0,1:T(8,128)}) %all-reduce.10.cloned.1.call-update) | async-done | bytes 262160 | tf_op jit(solution)/shard_map/psum | solution.py:27
  1502.4 11.7 cholesky.172
  1514.1 9.8 custom-call.15
  1524.4 11.7 cholesky.189
  1543.4 19.7 custom-call.16
  1579.2 23.5 fusion.5
  1602.8 49.1 %reduce-scatter.4.cloned.1.call-done = f32[512,256]{1,0:T(8,128)} async-done(((f32[4096,256]{1,0:T(8,128)}), f32[512,256]{1,0:T(8,128)}) %reduce-scatter.4.cloned.1.call-update) | async-done | bytes 524304 | tf_op jit(solution)/shard_map/reduce_scatter | solution.py:52
  1653.7 27.8 %all-gather.6.cloned.1.call-done = bf16[4096,256]{1,0:T(8,128)(2,1)} async-done(((bf16[512,256]{1,0:T(8,128)(2,1)}), bf16[4096,256]{1,0:T(8,128)(2,1)}) %all-gather.6.cloned.1.call-update) | async-done | bytes 2097168 | tf_op jit(solution)/shard_map/all_gather | solution.py:60
  1681.5 25.8 %fusion.46 = f32[6656,256]{1,0:T(8,128)} fusion(bf16[4096,6656]{1,0:T(8,128)(2,1)} %bitcast.8, bf16[4096,256]{1,0:T(8,128)(2,1)} %all-gather.6.cloned.1.call-done), kind=kOutput, calls=%fused_computation.101 | convolution fusion | flops 13958643712 | bytes 63438848 | tf_op jit(solution)/shard_map/dot_general | solution.py:43
  1707.4 146.3 %all-reduce.12.cloned.1.call-done = f32[6656,256]{1,0:T(8,128)} async-done(((f32[6656,256]{1,0:T(8,128)}), f32[6656,256]{1,0:T(8,128)}) %all-reduce.12.cloned.1.call-update) | async-done | bytes 6815760 | tf_op jit(solution)/shard_map/psum | solution.py:49
  1853.7 16.6 fusion.47
  1870.8 55.1 %all-reduce.14.cloned.1.call-done = f32[256,256]{0,1:T(8,128)} async-done(((f32[256,256]{0,1:T(8,128)}), f32[256,256]{0,1:T(8,128)}) %all-reduce.14.cloned.1.call-update) | async-done | bytes 262160 | tf_op jit(solution)/shard_map/psum | solution.py:27
  1928.0 11.7 cholesky.206
  1950.1 11.7 cholesky.223
  1969.3 19.7 custom-call.18
  2005.4 23.5 fusion.4
  2028.9 49.1 %reduce-scatter.6.cloned.1.call-done = f32[512,256]{1,0:T(8,128)} async-done(((f32[4096,256]{1,0:T(8,128)}), f32[512,256]{1,0:T(8,128)}) %reduce-scatter.6.cloned.1.call-update) | async-done | bytes 524304 | tf_op jit(solution)/shard_map/reduce_scatter | solution.py:52
  2079.9 28.0 %all-gather.8.cloned.1.call-done = bf16[4096,256]{1,0:T(8,128)(2,1)} async-done(((bf16[512,256]{1,0:T(8,128)(2,1)}), bf16[4096,256]{1,0:T(8,128)(2,1)}) %all-gather.8.cloned.1.call-update) | async-done | bytes 2097168 | tf_op jit(solution)/shard_map/all_gather | solution.py:60
  2107.8 25.8 %fusion.48 = f32[6656,256]{1,0:T(8,128)} fusion(bf16[4096,6656]{1,0:T(8,128)(2,1)} %bitcast.8, bf16[4096,256]{1,0:T(8,128)(2,1)} %all-gather.8.cloned.1.call-done), kind=kOutput, calls=%fused_computation.103 | convolution fusion | flops 13958643712 | bytes 63438848 | tf_op jit(solution)/shard_map/dot_general | solution.py:43
  2133.8 146.3 %all-reduce.16.cloned.1.call-done = f32[6656,256]{1,0:T(8,128)} async-done(((f32[6656,256]{1,0:T(8,128)}), f32[6656,256]{1,0:T(8,128)}) %all-reduce.16.cloned.1.call-update) | async-done | bytes 6815760 | tf_op jit(solution)/shard_map/psum | solution.py:49
  2280.0 16.6 fusion.49
  2296.9 55.3 %all-reduce.18.cloned.1.call-done = f32[256,256]{0,1:T(8,128)} async-done(((f32[256,256]{0,1:T(8,128)}), f32[256,256]{0,1:T(8,128)}) %all-reduce.18.cloned.1.call-update) | async-done | bytes 262160 | tf_op jit(solution)/shard_map/psum | solution.py:27
  2354.3 11.7 cholesky.240
  2376.4 11.7 cholesky.257
  2395.5 19.9 custom-call.20
  2432.1 24.9 fusion.2
  2470.5 35.7 %reduce-scatter.8.cloned.1.call-done = f32[512,256]{1,0:T(8,128)} async-done(((f32[4096,256]{1,0:T(8,128)}), f32[512,256]{1,0:T(8,128)}) %reduce-scatter.8.cloned.1.call-update) | async-done | bytes 524304 | tf_op jit(solution)/shard_map/reduce_scatter | solution.py:52
  (118 shorter events, 184.6 us)
Async XLA Ops:
  56.7 1199.1 %all-to-all-start = ((bf16[8,512,6656]{2,1,0:T(8,128)(2,1)}), bf16[8,512,6656]{2,1,0:T(8,128)(2,1)}, u32[]{:S(2)}, u32[]{:S(2)}) async-start(bf16[8,512,6656]{2,1,0:T(8,128)(2,1)} %bitcast_dynamic-update-slice_fusion.3), calls=%async_computation | async-start | bytes 109051904 | tf_op jit(solution)/shard_map/all_to_all | solution.py:32
  65.5 52.0 %all-gather.4.cloned.1.call-start = ((), (), s32[]{:S(2)}) async-start(), calls=%async_computation.4 | async-start | bytes 2359296 | tf_op jit(solution)/shard_map/all_gather | solution.py:47
  66.2 1361.9 %all-reduce.8.cloned.1.call-start = ((), (), s32[]{:S(2)}) async-start(), calls=%async_computation.5 | async-start | bytes 13631488 | tf_op jit(solution)/shard_map/psum | solution.py:49
  1281.6 218.7 %all-reduce.10.cloned.1.call-start = ((), (), s32[]{:S(2)}) async-start(), calls=%async_computation.6 | async-start | bytes 524288 | tf_op jit(solution)/shard_map/psum | solution.py:27
  1444.7 207.1 %reduce-scatter.4.cloned.1.call-start = ((), (), s32[]{:S(2)}) async-start(), calls=%async_computation.7 | async-start | bytes 4718592 | tf_op jit(solution)/shard_map/reduce_scatter | solution.py:52
  1542.7 0.7 copy-start.4
  1563.0 5.2 copy-start
  1602.7 78.8 %all-gather.6.cloned.1.call-start = ((), (), s32[]{:S(2)}) async-start(), calls=%async_computation.8 | async-start | bytes 2359296 | tf_op jit(solution)/shard_map/all_gather | solution.py:60
  1653.6 200.1 %all-reduce.12.cloned.1.call-start = ((), (), s32[]{:S(2)}) async-start(), calls=%async_computation.9 | async-start | bytes 13631488 | tf_op jit(solution)/shard_map/psum | solution.py:49
  1707.4 218.5 %all-reduce.14.cloned.1.call-start = ((), (), s32[]{:S(2)}) async-start(), calls=%async_computation.10 | async-start | bytes 524288 | tf_op jit(solution)/shard_map/psum | solution.py:27
  1870.3 207.7 %reduce-scatter.6.cloned.1.call-start = ((), (), s32[]{:S(2)}) async-start(), calls=%async_computation.11 | async-start | bytes 4718592 | tf_op jit(solution)/shard_map/reduce_scatter | solution.py:52
  1968.6 0.7 copy-start.5
  1989.0 5.2 copy-start.2
  2028.9 78.9 %all-gather.8.cloned.1.call-start = ((), (), s32[]{:S(2)}) async-start(), calls=%async_computation.12 | async-start | bytes 2359296 | tf_op jit(solution)/shard_map/all_gather | solution.py:60
  2079.8 200.2 %all-reduce.16.cloned.1.call-start = ((), (), s32[]{:S(2)}) async-start(), calls=%async_computation.13 | async-start | bytes 13631488 | tf_op jit(solution)/shard_map/psum | solution.py:49
  2133.7 218.5 %all-reduce.18.cloned.1.call-start = ((), (), s32[]{:S(2)}) async-start(), calls=%async_computation.14 | async-start | bytes 524288 | tf_op jit(solution)/shard_map/psum | solution.py:27
  2296.7 209.5 %reduce-scatter.8.cloned.1.call-start = ((), (), s32[]{:S(2)}) async-start(), calls=%async_computation.15 | async-start | bytes 4718592 | tf_op jit(solution)/shard_map/reduce_scatter | solution.py:52
  2394.8 0.7 copy-start.3
  2415.4 5.2 copy-start.1
Sparse Core Ops, SparseCore 0:
  67.9 49.5 all-gather.3
  1281.7 146.3 all-reduce.7
  1444.8 55.4 all-reduce.9
  1602.8 48.9 reduce-scatter.3
  1653.9 27.6 all-gather.5
  1707.5 146.1 all-reduce.11
  1870.5 55.4 all-reduce.13
  2029.0 48.9 reduce-scatter.5
  2080.2 27.5 all-gather.7
  2133.8 146.1 all-reduce.15
  2296.8 55.4 all-reduce.17
  2457.1 48.9 reduce-scatter.7
